TPU v7x, 32 devices: a whole 2x2x4 slice. The times are simulated.
32 devices in a mesh: req: 2 (over x), seq: 16 (over z, y, core).
Axes of the slice: x: 2, y: 2, z: 4, core: 2. Of those that a mesh axis runs over, the one named last changes fastest.
Arguments:
- states: bfloat16 [4, 4, 4544], P(None, 'req', 'seq'), may hold values from -6 to 6
- kv_cache: bfloat16 [4, 8192, 128], P('req', 'seq'), may hold values from -48 to 48, as said below
- lengths: int32 [4], replicated, may hold values from 1 to 8188, as said below
- placement: int32 [4], replicated, may hold values from 0 to 3, each once
- norm_gain: bfloat16 [4544], replicated, may hold values from 0.25 to 1.75
- norm_bias: bfloat16 [4544], replicated, may hold values from -1.5 to 1.5
- w_query: bfloat16 [4544, 4544], P('req', 'seq'), may hold values from -0.09375 to 0.09375
- w_keyval: bfloat16 [4544, 128], P('req'), may hold values from -0.09375 to 0.09375
- w_out: bfloat16 [4544, 4544], P('seq', 'req'), may hold values from -0.09375 to 0.09375
- w_up: bfloat16 [4544, 18176], P('req', 'seq'), may hold values from -0.09375 to 0.09375
- w_down: bfloat16 [18176, 4544], P('seq', 'req'), may hold values from -0.046875 to 0.046875
Outputs:
- new_states: bfloat16 [4, 4, 4544], P(None, 'req', 'seq')
- new_cache: bfloat16 [4, 8192, 128], P('req', 'seq')
Inputs may be any that keep to these rules, and one draw needn't show every extreme that they name: Request r's cache holds its first lengths[r] positions; some request has exactly 8188. `kv_cache`: row i is the cache of request placement[i]; positions at or beyond that request's length hold arbitrary values. `placement`: each request is served by exactly one slot.
All inputs are finite; a program needn't handle non-finite values.
Results may differ from a plain program's by a relative error of at most 0.012.
The roundings to bfloat16 on the way count: a program that leaves them out, or rounds other values in their place, can miss the bound.
Values may be sent and summed in bfloat16 or wider, within the bound.
No kernel may reach another device: no remote copies, remote signals or barrier semaphores. Data moves between devices by JAX's collectives and lax.ppermute only.
A program may use at most 192 MiB of HBM per device.

v0:
```python
import jax
import jax.numpy as jnp
from jax import lax
from jax.sharding import PartitionSpec as P

STEPS = 4
EPSILON = 1e-05
NEGATIVE = -1e30


def joined_2(part, axis, combine):
    gathered = jax.tree.map(lambda a: lax.all_gather(a, axis), part)

    def take(source):
        return jax.tree.map(lambda a: lax.dynamic_index_in_dim(a, source, 0, False), gathered)

    return lax.fori_loop(
        1, lax.axis_size(axis), lambda source, state: combine(state, take(source)), take(0)
    )


def layer_norm(row_block, norm_gain, norm_bias):
    values = row_block.astype(jnp.float32)
    average = jnp.mean(values, axis=-1, keepdims=True)
    centered = values - average
    spread = jnp.mean(centered * centered, axis=-1, keepdims=True)
    scaled = centered * lax.rsqrt(spread + EPSILON)
    return (scaled * norm_gain.astype(jnp.float32) + norm_bias.astype(jnp.float32)).astype(
        jnp.bfloat16
    )


def rotate(vectors, positions):
    head_width = vectors.shape[-1]
    half_width = head_width // 2
    frequency = 10000.0 ** (-(jnp.arange(half_width, dtype=jnp.float32) * 2.0) / head_width)
    angles = positions.astype(jnp.float32)[:, None] * frequency[None, :]
    cosine = jnp.concatenate([jnp.cos(angles), jnp.cos(angles)], axis=-1)[:, None, :]
    sine_wave = jnp.concatenate([jnp.sin(angles), jnp.sin(angles)], axis=-1)[:, None, :]
    turned = jnp.concatenate([-vectors[..., half_width:], vectors[..., :half_width]], axis=-1)
    return vectors * cosine + turned * sine_wave


def combine_parts(earlier, later):
    peak_first, total_first, weighted_first = earlier
    peak_second, total_second, weighted_second = later
    peak_score = jnp.maximum(peak_first, peak_second)
    scale_first = jnp.exp(peak_first - peak_score)
    scale_second = jnp.exp(peak_second - peak_score)
    weight_total = total_first * scale_first + total_second * scale_second
    weighted = weighted_first * scale_first[:, :, None] + weighted_second * scale_second[:, :, None]
    return (peak_score, weight_total, weighted)


def shards(
    states,
    kv_cache,
    lengths,
    placement,
    norm_gain,
    norm_bias,
    w_query,
    w_keyval,
    w_out,
    w_up,
    w_down,
):
    group_rows = kv_cache.shape[0]
    seg_length = kv_cache.shape[1]
    head_width = kv_cache.shape[2] // 2
    model_width = norm_gain.shape[0]
    head_count = model_width // head_width
    slice_width = states.shape[2]
    group_index = lax.axis_index("req")
    shard_index = lax.axis_index("seq")
    own_requests = lax.dynamic_slice_in_dim(placement, group_index * group_rows, group_rows, 0)
    slot_lengths = jnp.take(lengths, own_requests)
    every_request = lax.all_gather(states, "req", axis=1, tiled=True)
    own_states = jnp.take(every_request, own_requests, axis=1)
    full_states = lax.all_gather(own_states, "seq", axis=2, tiled=True)
    query_cols, keyval_cols, up_cols, out_rows, down_rows = (
        lax.all_gather(w_query, "req", axis=0, tiled=True),
        lax.all_gather(w_keyval, "req", axis=0, tiled=True),
        lax.all_gather(w_up, "req", axis=0, tiled=True),
        lax.all_gather(w_out, "req", axis=1, tiled=True),
        lax.all_gather(w_down, "req", axis=1, tiled=True),
    )
    first_matrix = jnp.concatenate([query_cols, keyval_cols, up_cols], axis=1)
    second_matrix = jnp.concatenate([out_rows, down_rows], axis=0)
    local_slots = jnp.arange(seg_length, dtype=jnp.int32)
    global_positions = shard_index * seg_length + local_slots
    cache_now = kv_cache
    outputs = []
    for step_index in range(STEPS):
        current = own_states[step_index]
        normed = layer_norm(full_states[step_index], norm_gain, norm_bias)
        first_out = jnp.dot(normed, first_matrix, preferred_element_type=jnp.float32)
        query_part = first_out[:, :slice_width].astype(jnp.bfloat16)
        keyval = first_out[:, slice_width : slice_width + 2 * head_width]
        up_part = first_out[:, slice_width + 2 * head_width :]
        positions = slot_lengths + step_index
        query_all = lax.all_gather(query_part, "seq", axis=1, tiled=True)
        query_rows = rotate(
            query_all.astype(jnp.float32).reshape(group_rows, head_count, head_width), positions
        ).astype(jnp.bfloat16)
        new_key = rotate(keyval[:, None, :head_width], positions)[:, 0, :]
        new_entry = jnp.concatenate([new_key, keyval[:, head_width:]], axis=-1).astype(jnp.bfloat16)
        write_mask = local_slots[None, :] == (positions - shard_index * seg_length)[:, None]
        cache_now = jnp.where(write_mask[:, :, None], new_entry[:, None, :], cache_now)
        key_rows = cache_now[:, :, :head_width]
        value_rows = cache_now[:, :, head_width:]
        scores = jnp.einsum(
            "ghd,gsd->ghs", query_rows, key_rows, preferred_element_type=jnp.float32
        ) * head_width ** (-0.5)
        valid_mask = (global_positions[None, :] <= positions[:, None])[:, None, :]
        highest = jnp.max(jnp.where(valid_mask, scores, NEGATIVE), axis=-1)
        weights = jnp.where(valid_mask, jnp.exp(scores - highest[:, :, None]), 0.0)
        weight_total = jnp.sum(weights, axis=-1)
        weighted = jnp.einsum(
            "ghs,gsd->ghd", weights, value_rows, preferred_element_type=jnp.float32
        )
        peak_score, denominator, numerator = joined_2(
            (highest, weight_total, weighted), "seq", combine_parts
        )
        mixed_all = (
            (numerator / denominator[:, :, None])
            .reshape(group_rows, model_width)
            .astype(jnp.bfloat16)
        )
        mixed_part = lax.dynamic_slice_in_dim(mixed_all, shard_index * slice_width, slice_width, 1)
        hidden = jax.nn.gelu(up_part, approximate=False).astype(jnp.bfloat16)
        joined = jnp.concatenate([mixed_part, hidden], axis=1)
        partial_sum = jnp.dot(joined, second_matrix, preferred_element_type=jnp.float32)
        update = lax.psum_scatter(partial_sum, "seq", scatter_dimension=1, tiled=True)
        outputs.append((current.astype(jnp.float32) + update).astype(jnp.bfloat16))
    stacked = jnp.stack(outputs)
    slot_states = lax.all_gather(stacked, "req", axis=1, tiled=True)
    request_total = placement.shape[0]
    inverse = (
        jnp.zeros((request_total,), jnp.int32)
        .at[placement]
        .set(jnp.arange(request_total, dtype=jnp.int32))
    )
    own_inverse = lax.dynamic_slice_in_dim(inverse, group_index * group_rows, group_rows, 0)
    return (jnp.take(slot_states, own_inverse, axis=1), cache_now)


def solution(mesh):
    in_specs = (
        P(None, "req", "seq"),
        P("req", "seq", None),
        P(),
        P(),
        P(),
        P(),
        P("req", "seq"),
        P("req", None),
        P("seq", "req"),
        P("req", "seq"),
        P("seq", "req"),
    )
    out_specs = (P(None, "req", "seq"), P("req", "seq", None))
    return jax.shard_map(shards, mesh=mesh, in_specs=in_specs, out_specs=out_specs, check_vma=False)
```

profile of v0, /device:TPU:8, one launch (start us, length us, event | category | flops | bytes accessed | tf_op | source)
XLA Modules:
  0.0 748.7 jit_solution(15381080556855086247)
XLA Ops:
  7.2 0.7 all-gather.40.cloned.1.call-update
  8.0 0.7 all-gather.38.cloned.1.call-update
  8.7 0.7 all-gather.32.cloned.1.call-update
  10.0 8.6 %copy.124 = bf16[1136,2272]{0,1:T(8,128)(2,1)} copy(bf16[1136,2272]{1,0:T(8,128)(2,1)} %param.31) | data formatting | bytes 10323968 | tf_op args[10]
  18.7 4.4 all_gather.108
  24.0 30.8 %all_gather.109 = bf16[4,2,4544]{0,1,2:T(2,128)(2,1)S(1)} all-gather(bf16[4,2,284]{0,1,2:T(2,128)(2,1)S(1)} %copy.114), channel_id=1, replica_groups=mesh['req'=2,'seq'=16] {'seq'}, dimensions={2}, use_global_device_ids=true | all-gather | bytes 77248 | tf_op jit(solution)/shard_map/all_gather | solution.py:80
  54.8 10.2 %fusion.177 = (bf16[1,2,4544]{0,1,2:T(2,128)(2,1)S(1)}, bf16[1,2,4544]{0,1,2:T(2,128)(2,1)}, f32[1,2,4544]{0,1,2:T(2,128)}, bf16[1,2,4544]{0,1,2:T(2,128)(2,1)}) fusion(bf16[4,2,4544]{0,1,2:T(2,128)(2,1)S(1)} %all_gather.109), kind=kLoop, calls=%fused_computation.365 | loop fusion | flops 9088 | bytes 163584 | tf_op jit(solution)/shard_map/slice | solution.py:96
  65.0 5.3 fusion.48
  70.3 0.6 fusion.178
  70.9 5.5 copy.138
  77.3 0.6 gather_fusion
  77.9 5.1 copy.167
  84.1 5.1 copy.166
  90.2 0.9 copy.119
  91.1 2.4 copy.165
  95.0 0.6 compare_and_fusion
  95.6 0.7 iota_compare_fusion
  96.3 0.7 iota_compare_fusion.2
  96.9 0.6 dynamic-slice
  98.2 0.7 broadcast_compare_fusion.3
  98.9 0.7 multiply_cosine_fusion.3
  99.6 6.0 copy.123
  105.7 6.1 reshape.547
  111.8 3.0 copy.125
  114.7 3.9 copy.150
  118.7 127.5 %all-gather.34.cloned.1.call-done = bf16[4544,1136]{1,0:T(8,128)(2,1)} async-done(((bf16[2272,1136]{1,0:T(8,128)(2,1)}), bf16[4544,1136]{1,0:T(8,128)(2,1)}) %all-gather.34.cloned.1.call-update) | async-done | bytes 10323984 | tf_op jit(solution)/shard_map/all_gather | solution.py:84
  246.2 25.5 %concatenate.126 = bf16[4544,1548]{1,0:T(8,128)(2,1)} concatenate(bf16[4544,284]{1,0:T(8,128)(2,1)S(1)} %bitcast.276, bf16[4544,128]{1,0:T(8,128)(2,1)} %all-gather.32.cloned.1.call-done, bf16[4544,1136]{1,0:T(8,128)(2,1)} %all-gather.34.cloned.1.call-done), dimensions={1} | concatenate | bytes 28136448 | tf_op jit(solution)/shard_map/concatenate | solution.py:88
  271.8 7.6 %fusion.179 = (bf16[2,1548]{1,0:T(2,128)(2,1)S(1)}, f32[2,1548]{1,0:T(2,128)S(1)}) fusion(bf16[4544,1548]{1,0:T(8,128)(2,1)} %concatenate.126, f32[1,2,4544]{2,1,0:T(2,128)} %copy-done.6, f32[2]{0:T(128)} %add_rsqrt_fusion, f32[2]{0:T(128)} %copy-done.26, f32[4544]{0:T(1024)S(1)} %convert_element_type.189, f32[4544]{0:T(1024)S(1)} %convert_element_type.188), kind=kOutput, calls=%fused_computation.367 | convolution fusion | flops 28184984 | bytes 14159520 | tf_op jit(solution)/shard_map/dot_general | solution.py:97
  279.6 1.8 copy-done.2
  281.4 2.1 fusion.180
  283.8 2.1 fusion.181
  286.3 2.1 fusion.182
  288.6 18.7 %all-gather.23 = bf16[16,284,2]{1,2,0:T(2,128)(2,1)S(1)} all-gather(bf16[1,284,2]{1,2,0:T(2,128)(2,1)S(1)} %slice_bitcast_fusion), channel_id=1, replica_groups=mesh['req'=2,'seq'=16] {'seq'}, dimensions={0}, use_global_device_ids=true | all-gather | bytes 19312 | tf_op jit(solution)/shard_map/all_gather | solution.py:102
  309.5 17.5 %all-gather.20 = bf16[16,284,2]{1,2,0:T(2,128)(2,1)S(1)} all-gather(bf16[1,284,2]{1,2,0:T(2,128)(2,1)S(1)} %slice_bitcast_fusion.1), channel_id=1, replica_groups=mesh['req'=2,'seq'=16] {'seq'}, dimensions={0}, use_global_device_ids=true | all-gather | bytes 19312 | tf_op jit(solution)/shard_map/all_gather | solution.py:102
  328.1 19.0 %all-gather.17 = bf16[16,284,2]{1,2,0:T(2,128)(2,1)S(1)} all-gather(bf16[1,284,2]{1,2,0:T(2,128)(2,1)S(1)} %slice_bitcast_fusion.2), channel_id=1, replica_groups=mesh['req'=2,'seq'=16] {'seq'}, dimensions={0}, use_global_device_ids=true | all-gather | bytes 19312 | tf_op jit(solution)/shard_map/all_gather | solution.py:102
  348.3 17.5 %all-gather.13 = bf16[16,284,2]{1,2,0:T(2,128)(2,1)S(1)} all-gather(bf16[1,284,2]{1,2,0:T(2,128)(2,1)S(1)} %slice_bitcast_fusion.3), channel_id=1, replica_groups=mesh['req'=2,'seq'=16] {'seq'}, dimensions={0}, use_global_device_ids=true | all-gather | bytes 19312 | tf_op jit(solution)/shard_map/all_gather | solution.py:102
  367.0 18.8 %all-gather.24 = f32[16,2,71]{2,1,0:T(2,128)S(1)} all-gather(f32[1,2,71]{2,1,0:T(2,128)S(1)} %bitcast.291), channel_id=11, replica_groups=mesh['req'=2,'seq'=16] {'seq'}, dimensions={0}, use_global_device_ids=true | all-gather | bytes 9656 | tf_op jit(solution)/shard_map/all_gather | solution.py:12
  385.8 17.4 %all-gather.25 = f32[16,2,71]{2,1,0:T(2,128)S(1)} all-gather(f32[1,2,71]{2,1,0:T(2,128)S(1)} %bitcast.295), channel_id=12, replica_groups=mesh['req'=2,'seq'=16] {'seq'}, dimensions={0}, use_global_device_ids=true | all-gather | bytes 9656 | tf_op jit(solution)/shard_map/all_gather | solution.py:12
  403.2 22.0 %all-gather.11 = f32[32,71,64]{1,2,0:T(8,128)S(1)} all-gather(f32[2,71,64]{1,2,0:T(8,128)S(1)} %fusion.18), channel_id=13, replica_groups=mesh['req'=2,'seq'=16] {'seq'}, dimensions={0}, use_global_device_ids=true | all-gather | bytes 617984 | tf_op jit(solution)/shard_map/all_gather | solution.py:12
  425.3 4.4 while.79
  430.0 17.9 %all-gather.21 = f32[16,2,71]{2,1,0:T(2,128)S(1)} all-gather(f32[1,2,71]{2,1,0:T(2,128)S(1)} %bitcast.290), channel_id=8, replica_groups=mesh['req'=2,'seq'=16] {'seq'}, dimensions={0}, use_global_device_ids=true | all-gather | bytes 9656 | tf_op jit(solution)/shard_map/all_gather | solution.py:12
  447.8 18.2 %all-gather.22 = f32[16,2,71]{2,1,0:T(2,128)S(1)} all-gather(f32[1,2,71]{2,1,0:T(2,128)S(1)} %bitcast.294), channel_id=9, replica_groups=mesh['req'=2,'seq'=16] {'seq'}, dimensions={0}, use_global_device_ids=true | all-gather | bytes 9656 | tf_op jit(solution)/shard_map/all_gather | solution.py:12
  466.0 21.3 %all-gather.8 = f32[32,71,64]{1,2,0:T(8,128)S(1)} all-gather(f32[2,71,64]{1,2,0:T(8,128)S(1)} %fusion.16), channel_id=10, replica_groups=mesh['req'=2,'seq'=16] {'seq'}, dimensions={0}, use_global_device_ids=true | all-gather | bytes 617984 | tf_op jit(solution)/shard_map/all_gather | solution.py:12
  487.4 4.4 while.78
  492.0 18.3 %all-gather.18 = f32[16,2,71]{2,1,0:T(2,128)S(1)} all-gather(f32[1,2,71]{2,1,0:T(2,128)S(1)} %bitcast.289), channel_id=5, replica_groups=mesh['req'=2,'seq'=16] {'seq'}, dimensions={0}, use_global_device_ids=true | all-gather | bytes 9656 | tf_op jit(solution)/shard_map/all_gather | solution.py:12
  510.3 17.8 %all-gather.19 = f32[16,2,71]{2,1,0:T(2,128)S(1)} all-gather(f32[1,2,71]{2,1,0:T(2,128)S(1)} %bitcast.293), channel_id=6, replica_groups=mesh['req'=2,'seq'=16] {'seq'}, dimensions={0}, use_global_device_ids=true | all-gather | bytes 9656 | tf_op jit(solution)/shard_map/all_gather | solution.py:12
  528.0 21.7 %all-gather.5 = f32[32,71,64]{1,2,0:T(8,128)S(1)} all-gather(f32[2,71,64]{1,2,0:T(8,128)S(1)} %fusion.14), channel_id=7, replica_groups=mesh['req'=2,'seq'=16] {'seq'}, dimensions={0}, use_global_device_ids=true | all-gather | bytes 617984 | tf_op jit(solution)/shard_map/all_gather | solution.py:12
  549.8 4.4 while.77
  554.5 18.0 %all-gather.14 = f32[16,2,71]{2,1,0:T(2,128)S(1)} all-gather(f32[1,2,71]{2,1,0:T(2,128)S(1)} %bitcast.288), channel_id=2, replica_groups=mesh['req'=2,'seq'=16] {'seq'}, dimensions={0}, use_global_device_ids=true | all-gather | bytes 9656 | tf_op jit(solution)/shard_map/all_gather | solution.py:12
  572.5 18.0 %all-gather.15 = f32[16,2,71]{2,1,0:T(2,128)S(1)} all-gather(f32[1,2,71]{2,1,0:T(2,128)S(1)} %bitcast.292), channel_id=3, replica_groups=mesh['req'=2,'seq'=16] {'seq'}, dimensions={0}, use_global_device_ids=true | all-gather | bytes 9656 | tf_op jit(solution)/shard_map/all_gather | solution.py:12
  590.5 21.5 %all-gather.2 = f32[32,71,64]{1,2,0:T(8,128)S(1)} all-gather(f32[2,71,64]{1,2,0:T(8,128)S(1)} %fusion.12), channel_id=4, replica_groups=mesh['req'=2,'seq'=16] {'seq'}, dimensions={0}, use_global_device_ids=true | all-gather | bytes 617984 | tf_op jit(solution)/shard_map/all_gather | solution.py:12
  612.0 4.4 while.76
  617.7 10.7 %fusion.136 = f32[2,4544]{1,0:T(2,128)} fusion(bf16[2,1136]{1,0:T(2,128)(2,1)S(1)} %fusion.115, bf16[2,284]{1,0:T(2,128)(2,1)S(1)} %constant_dynamic-slice_fusion.8, bf16[1136,4544]{0,1:T(8,128)(2,1)} %all-gather.36.cloned.1.call-done, bf16[284,4544]{0,1:T(8,128)(2,1)} %copy.125), kind=kOutput, calls=%fused_computation.232 | convolution fusion | flops 51631200 | bytes 12946992 | tf_op jit(solution)/shard_map/dot_general | solution.py:133
  628.4 4.8 fusion.132
  633.2 4.8 fusion.128
  638.1 4.8 fusion.124
  642.9 1.8 copy.145
  644.7 88.3 %all-reduce.7.cloned.1.call-done = (f32[2,4544]{1,0:T(2,128)}, f32[2,4544]{1,0:T(2,128)}, f32[2,4544]{1,0:T(2,128)}, f32[2,4544]{1,0:T(2,128)}) async-done(((f32[2,4544]{1,0:T(2,128)}, f32[2,4544]{1,0:T(2,128)}, f32[2,4544]{1,0:T(2,128)}, f32[2,4544]{1,0:T(2,128)}), (f32[2,4544]{1,0:T(2,128)}, f32[2,4544]{1,0:T(2,128)}, f32[2,4544]{1,0:T(2,128)}, f32[2,4544]{1,0:T(2,128)})) %all-reduce.7.cloned.1.call-update) | async-done | bytes 145424
  733.0 0.8 fusion.147
  733.7 0.8 fusion.146
  734.5 0.8 fusion.145
  735.3 0.8 fusion.144
  736.1 4.4 all_gather.143
  741.1 0.6 copy.144
  (470 shorter events, 31.1 us)
Async XLA Ops:
  7.2 70.1 %copy-start = (s32[4]{0:T(128)S(1)}, s32[4]{0:T(128)}, u32[]{:S(2)}) copy-start(s32[4]{0:T(128)} %param.23) | copy-start | bytes 52
  7.2 92.4 %all-gather.40.cloned.1.call-start = ((), (), s32[]{:S(2)}) async-start(), calls=%async_computation.4 | async-start | bytes 3981312 | tf_op jit(solution)/shard_map/all_gather | solution.py:85
  7.9 106.8 %all-gather.38.cloned.1.call-start = ((), (), s32[]{:S(2)}) async-start(), calls=%async_computation.3 | async-start | bytes 3981312 | tf_op jit(solution)/shard_map/all_gather | solution.py:82
  8.7 110.0 %all-gather.32.cloned.1.call-start = ((), (), s32[]{:S(2)}) async-start(), calls=%async_computation | async-start | bytes 1744896 | tf_op jit(solution)/shard_map/all_gather | solution.py:83
  9.4 9.3 %copy-start.25 = (bf16[4,2,284]{2,1,0:T(2,128)(2,1)S(1)}, bf16[4,2,284]{2,1,0:T(2,128)(2,1)}, u32[]{:S(2)}) copy-start(bf16[4,2,284]{2,1,0:T(2,128)(2,1)} %param.21) | copy-start | bytes 13636
  9.4 13.7 %copy-start.46 = (s32[4]{0:T(128)S(1)}, s32[4]{0:T(128)}, u32[]{:S(2)}) copy-start(s32[4]{0:T(128)} %param.24) | copy-start | bytes 52
  9.4 236.8 %all-gather.34.cloned.1.call-start = ((), (), s32[]{:S(2)}) async-start(), calls=%async_computation.1 | async-start | bytes 15704064 | tf_op jit(solution)/shard_map/all_gather | solution.py:84
  10.0 607.7 %all-gather.36.cloned.1.call-start = ((), (), s32[]{:S(2)}) async-start(), calls=%async_computation.2 | async-start | bytes 15704064 | tf_op jit(solution)/shard_map/all_gather | solution.py:86
  18.7 714.3 %all-reduce.7.cloned.1.call-start = ((), (), s32[]{:S(2)}) async-start(), calls=%async_computation.5 | async-start | bytes 294912
  54.8 22.4 %copy-start.19 = (bf16[4544]{0:T(1024)(128)(2,1)S(1)}, bf16[4544]{0:T(1024)(128)(2,1)}, u32[]{:S(2)}) copy-start(bf16[4544]{0:T(1024)(128)(2,1)} %param.26) | copy-start | bytes 27268
  54.8 22.4 %copy-start.20 = (bf16[4544]{0:T(1024)(128)(2,1)S(1)}, bf16[4544]{0:T(1024)(128)(2,1)}, u32[]{:S(2)}) copy-start(bf16[4544]{0:T(1024)(128)(2,1)} %param.25) | copy-start | bytes 27268
  65.0 25.2 %copy-start.11 = (bf16[2,512,128]{2,1,0:T(8,128)(2,1)S(1)}, bf16[2,512,128]{2,1,0:T(8,128)(2,1)}, u32[]{:S(2)}) copy-start(bf16[2,512,128]{2,1,0:T(8,128)(2,1)} %param.22) | copy-start | bytes 786436
  65.0 31.9 %copy-start.48 = (u32[32]{0:T(128)S(1)}, u32[32]{0:T(128)}, u32[]{:S(2)}) copy-start(u32[32]{0:T(128)} %constant.327) | copy-start | bytes 388
  76.4 23.2 %copy-start.6 = (f32[1,2,4544]{2,1,0:T(2,128)}, f32[1,2,4544]{2,1,0:T(2,128)S(1)}, u32[]{:S(2)}) copy-start(f32[1,2,4544]{2,1,0:T(2,128)S(1)} %copy.138) | copy-start | bytes 109060
  76.5 1.5 copy-start.26
  83.1 1.0 copy-start.9
  83.2 6.0 copy-start.31
  89.2 10.4 %copy-start.7 = (bf16[1,2,4544]{2,1,0:T(2,128)(2,1)}, bf16[1,2,4544]{2,1,0:T(2,128)(2,1)S(1)}, u32[]{:S(2)}) copy-start(bf16[1,2,4544]{2,1,0:T(2,128)(2,1)S(1)} %copy.166) | copy-start | bytes 54532
  89.4 4.1 copy-start.29
  93.6 4.6 copy-start.27
  271.8 9.6 %copy-start.2 = (bf16[4544,1548]{1,0:T(8,128)(2,1)S(1)}, bf16[4544,1548]{1,0:T(8,128)(2,1)}, u32[]{:S(2)}) copy-start(bf16[4544,1548]{1,0:T(8,128)(2,1)} %concatenate.126) | copy-start | bytes 42204676
  271.8 9.6 %copy-start.10 = (bf16[1,2,4544]{2,1,0:T(2,128)(2,1)S(1)}, bf16[1,2,4544]{2,1,0:T(2,128)(2,1)}, u32[]{:S(2)}) copy-start(bf16[1,2,4544]{2,1,0:T(2,128)(2,1)} %copy-done.9) | copy-start | bytes 54532
  271.8 9.6 %copy-start.32 = (f32[2]{0:T(128)S(1)}, f32[2]{0:T(128)}, u32[]{:S(2)}) copy-start(f32[2]{0:T(128)} %copy-done.31) | copy-start | bytes 28
  271.8 9.6 %copy-start.43 = (f32[2]{0:T(128)S(1)}, f32[2]{0:T(128)}, u32[]{:S(2)}) copy-start(f32[2]{0:T(128)} %add_rsqrt_fusion.1) | copy-start | bytes 28
  281.4 2.4 copy-start.8
  281.4 2.3 copy-start.30
  281.4 2.3 copy-start.42
  283.7 2.3 copy-start.28
  283.8 2.3 copy-start.41
  286.1 21.5 %copy-start.39 = (f32[2,32]{1,0:T(2,128)S(1)}, f32[2,32]{1,0:T(2,128)}, u32[]{:S(2)}) copy-start(f32[2,32]{1,0:T(2,128)} %get-tuple-element.1017) | copy-start | bytes 772
  286.1 21.5 %copy-start.40 = (f32[2,32]{1,0:T(2,128)S(1)}, f32[2,32]{1,0:T(2,128)}, u32[]{:S(2)}) copy-start(f32[2,32]{1,0:T(2,128)} %get-tuple-element.1018) | copy-start | bytes 772
  286.1 21.6 %copy-start.37 = (f32[2,32]{1,0:T(2,128)S(1)}, f32[2,32]{1,0:T(2,128)}, u32[]{:S(2)}) copy-start(f32[2,32]{1,0:T(2,128)} %get-tuple-element.1015) | copy-start | bytes 772
  286.1 21.6 %copy-start.38 = (f32[2,32]{1,0:T(2,128)S(1)}, f32[2,32]{1,0:T(2,128)}, u32[]{:S(2)}) copy-start(f32[2,32]{1,0:T(2,128)} %get-tuple-element.1016) | copy-start | bytes 772
  286.1 21.8 %copy-start.35 = (f32[2,32]{1,0:T(2,128)S(1)}, f32[2,32]{1,0:T(2,128)}, u32[]{:S(2)}) copy-start(f32[2,32]{1,0:T(2,128)} %get-tuple-element.1013) | copy-start | bytes 772
  286.2 21.8 %copy-start.36 = (f32[2,32]{1,0:T(2,128)S(1)}, f32[2,32]{1,0:T(2,128)}, u32[]{:S(2)}) copy-start(f32[2,32]{1,0:T(2,128)} %get-tuple-element.1014) | copy-start | bytes 772
  286.2 21.9 %copy-start.33 = (f32[2,32]{1,0:T(2,128)S(1)}, f32[2,32]{1,0:T(2,128)}, u32[]{:S(2)}) copy-start(f32[2,32]{1,0:T(2,128)} %get-tuple-element.987) | copy-start | bytes 772
  286.2 21.9 %copy-start.34 = (f32[2,32]{1,0:T(2,128)S(1)}, f32[2,32]{1,0:T(2,128)}, u32[]{:S(2)}) copy-start(f32[2,32]{1,0:T(2,128)} %get-tuple-element.988) | copy-start | bytes 772
  286.2 22.1 %copy-start.5 = (bf16[2,512,128]{1,2,0:T(8,128)(2,1)S(1)}, bf16[2,512,128]{1,2,0:T(8,128)(2,1)}, u32[]{:S(2)}) copy-start(bf16[2,512,128]{1,2,0:T(8,128)(2,1)} %copy.119) | copy-start | bytes 786436
  286.2 22.1 %copy-start.21 = (pred[2,512]{1,0:T(4,128)(4,1)S(1)}, pred[2,512]{1,0:T(4,128)(4,1)}, u32[]{:S(2)}) copy-start(pred[2,512]{1,0:T(4,128)(4,1)} %get-tuple-element.1035) | copy-start | bytes 3076
  286.2 22.0 %copy-start.22 = (pred[2,512]{1,0:T(4,128)(4,1)S(1)}, pred[2,512]{1,0:T(4,128)(4,1)}, u32[]{:S(2)}) copy-start(pred[2,512]{1,0:T(4,128)(4,1)} %get-tuple-element.1036) | copy-start | bytes 3076
  286.2 22.0 %copy-start.23 = (pred[2,512]{1,0:T(4,128)(4,1)S(1)}, pred[2,512]{1,0:T(4,128)(4,1)}, u32[]{:S(2)}) copy-start(pred[2,512]{1,0:T(4,128)(4,1)} %get-tuple-element.1037) | copy-start | bytes 3076
  286.2 22.0 %copy-start.24 = (pred[2,512]{1,0:T(4,128)(4,1)S(1)}, pred[2,512]{1,0:T(4,128)(4,1)}, u32[]{:S(2)}) copy-start(pred[2,512]{1,0:T(4,128)(4,1)} %get-tuple-element.1038) | copy-start | bytes 3076
  286.2 22.3 %copy-start.14 = (pred[2,512]{1,0:T(4,128)(4,1)S(1)}, pred[2,512]{1,0:T(4,128)(4,1)}, u32[]{:S(2)}) copy-start(pred[2,512]{1,0:T(4,128)(4,1)} %get-tuple-element.974) | copy-start | bytes 3076
  286.2 41.0 %copy-start.13 = (pred[2,512]{1,0:T(4,128)(4,1)S(1)}, pred[2,512]{1,0:T(4,128)(4,1)}, u32[]{:S(2)}) copy-start(pred[2,512]{1,0:T(4,128)(4,1)} %get-tuple-element.973) | copy-start | bytes 3076
  286.3 61.2 %copy-start.12 = (pred[2,512]{1,0:T(4,128)(4,1)S(1)}, pred[2,512]{1,0:T(4,128)(4,1)}, u32[]{:S(2)}) copy-start(pred[2,512]{1,0:T(4,128)(4,1)} %get-tuple-element.972) | copy-start | bytes 3076
  308.5 0.7 copy-start.4
  617.6 10.7 %copy-start.3 = (bf16[284,4544]{0,1:T(8,128)(2,1)S(1)}, bf16[284,4544]{0,1:T(8,128)(2,1)}, u32[]{:S(2)}) copy-start(bf16[284,4544]{0,1:T(8,128)(2,1)} %copy.125) | copy-start | bytes 7742980
  617.7 10.7 %copy-start.47 = (bf16[1136,4544]{0,1:T(8,128)(2,1)S(1)}, bf16[1136,4544]{0,1:T(8,128)(2,1)}, u32[]{:S(2)}) copy-start(bf16[1136,4544]{0,1:T(8,128)(2,1)} %all-gather.36.cloned.1.call-done) | copy-start | bytes 30971908
  633.2 108.5 %copy-start.1 = (s32[4]{0:T(128)S(1)}, s32[4]{0:T(128)}, u32[]{:S(2)}) copy-start(s32[4]{0:T(128)} %param.23) | copy-start | bytes 52
  638.0 4.9 copy-start.45
  638.0 94.9 %copy-start.18 = (f32[1,2,284]{2,0,1:T(1,128)S(1)}, f32[1,2,284]{2,0,1:T(1,128)}, u32[]{:S(2)}) copy-start(f32[1,2,284]{2,0,1:T(1,128)} %get-tuple-element.969) | copy-start | bytes 6820
  638.0 95.7 %copy-start.17 = (bf16[1,2,284]{2,0,1:T(2,128)(2,1)S(1)}, bf16[1,2,284]{2,0,1:T(2,128)(2,1)}, u32[]{:S(2)}) copy-start(bf16[1,2,284]{2,0,1:T(2,128)(2,1)} %get-tuple-element.970) | copy-start | bytes 3412
  638.0 96.5 %copy-start.16 = (bf16[1,2,284]{2,0,1:T(2,128)(2,1)S(1)}, bf16[1,2,284]{2,0,1:T(2,128)(2,1)}, u32[]{:S(2)}) copy-start(bf16[1,2,284]{2,0,1:T(2,128)(2,1)} %get-tuple-element.968) | copy-start | bytes 3412
  638.0 97.2 %copy-start.15 = (bf16[1,2,284]{2,0,1:T(2,128)(2,1)S(1)}, bf16[1,2,284]{2,0,1:T(2,128)(2,1)}, u32[]{:S(2)}) copy-start(bf16[1,2,284]{2,0,1:T(2,128)(2,1)} %get-tuple-element.967) | copy-start | bytes 3412
  638.1 102.9 %copy-start.44 = (pred[2]{0:T(512)(128)(4,1)S(1)}, pred[2]{0:T(512)(128)(4,1)}, u32[]{:S(2)}) copy-start(pred[2]{0:T(512)(128)(4,1)} %get-tuple-element.945) | copy-start | bytes 10
Sparse Core Ops, SparseCore 0:
  9.6 40.6 all-gather.39
  51.8 39.3 all-gather.37
  92.8 22.5 all-gather.31
  116.8 129.3 all-gather.33
  247.6 129.3 all-gather.35
  643.0 89.9 all-reduce.6
where the time goes:
time: 757 us; the launch traced here: 749 us
  blocking collectives  343 us (45%)
  waiting for transfers between devices  218 us (29%)
  local copies, waits for them, and re-layouts  89.1 us (12%)
  matrix products  41.4 us (5%)
  other arithmetic  38.8 us (5%)
  between operations  15.8 us (2%)
    all_gather x12, blocking collectives, joined_2(): gathered = jax.tree.map(lambda a: lax.all_gather(a, axis), part)  231 us
    all_gather x1, waiting for transfers between devices, shards(): lax.all_gather(w_up, 'req', axis=0, tiled=True)  128 us
    unnamed x7, waiting for transfers between devices  90.9 us
    all_gather x4, blocking collectives, shards(): query_all = lax.all_gather(query_part, 'seq', axis=1, tiled=True)  72.6 us
    unnamed x114, local copies, waits for them, and re-layouts  40.2 us
    all_gather x1, blocking collectives, shards(): full_states = lax.all_gather(own_states, 'seq', axis=2, tiled=True)  30.8 us
    concatenate x1, local copies, waits for them, and re-layouts, shards(): first_matrix = jnp.concatenate([query_cols, keyval_cols, up_cols], axis=1)  25.5 us
    dot_general x4, matrix products, shards(): jnp.dot(joined, second_matrix, preferred_element_type=jnp.float32)  25.1 us
  transfers between devices with their start and end apart: 6, of which 2 were waited for; matrix products, arithmetic and copies ran while one was open for 18% of the time, Pallas kernels for 0%

commit v1 on v0

--- a/solution.py
+++ b/solution.py
@@ -6,6 +6,19 @@
 STEPS = 4
 EPSILON = 1e-05
 NEGATIVE = -1e30
+
+
+def ring_gather(x, axis, dim):
+    ways = lax.axis_size(axis)
+    up = [(d, (d + 1) % ways) for d in range(ways)]
+    down = [(d, (d - 1) % ways) for d in range(ways)]
+    earlier, later = ([x], [x])
+    for _ in range(ways // 2):
+        earlier.append(lax.ppermute(earlier[-1], axis, up))
+    for _ in range((ways - 1) // 2):
+        later.append(lax.ppermute(later[-1], axis, down))
+    line = jnp.concatenate([*earlier[::-1], *later[1:]], axis=dim)
+    return jnp.roll(line, (lax.axis_index(axis) - ways // 2) * x.shape[dim], axis=dim)
 
 
 def joined_2(part, axis, combine):
@@ -99,7 +112,7 @@
         keyval = first_out[:, slice_width : slice_width + 2 * head_width]
         up_part = first_out[:, slice_width + 2 * head_width :]
         positions = slot_lengths + step_index
-        query_all = lax.all_gather(query_part, "seq", axis=1, tiled=True)
+        query_all = ring_gather(query_part, "seq", 1)
         query_rows = rotate(
             query_all.astype(jnp.float32).reshape(group_rows, head_count, head_width), positions
         ).astype(jnp.bfloat16)

time: 757 us -> 802 us (1.059)
  starting transfers between devices: 0.23 us -> 110 us
  blocking collectives: 343 us -> 276 us
    ppermute x0 -> x60, starting transfers between devices: none -> 110 us  [the longest x28 109 us: ring_gather(): later.append(lax.ppermute(later[-1], axis, down))]
    all_gather x4 -> x0, blocking collectives: 72.6 us -> none  [shards(): query_all = lax.all_gather(query_part, 'seq', axis=1, tiled=True)]
  transfers between devices with their start and end apart: 6 -> 66, of which waited for: 2 -> 4; matrix products, arithmetic and copies ran while one was open for 18% -> 18% of each run, Pallas kernels for 0% -> 0%
where the time goes in v1:
time: 802 us; the launch traced here: 796 us
  blocking collectives  276 us (34%)
  waiting for transfers between devices  222 us (28%)
  starting transfers between devices  110 us (14%)
  local copies, waits for them, and re-layouts  88.6 us (11%)
  matrix products  41.3 us (5%)
  other arithmetic  40.5 us (5%)
  between operations  16.4 us (2%)
    all_gather x12, blocking collectives, joined_2(): gathered = jax.tree.map(lambda a: lax.all_gather(a, axis), part)  236 us
    all_gather x1, waiting for transfers between devices, shards(): lax.all_gather(w_up, 'req', axis=0, tiled=True)  127 us
    ppermute x28, starting transfers between devices, ring_gather(): later.append(lax.ppermute(later[-1], axis, down))  109 us
    unnamed x7, waiting for transfers between devices  91.3 us
    unnamed x114, local copies, waits for them, and re-layouts  39.1 us
    all_gather x1, blocking collectives, shards(): full_states = lax.all_gather(own_states, 'seq', axis=2, tiled=True)  30.8 us
    concatenate x1, local copies, waits for them, and re-layouts, shards(): first_matrix = jnp.concatenate([query_cols, keyval_cols, up_cols], axis=1)  25.6 us
    dot_general x4, matrix products, shards(): jnp.dot(joined, second_matrix, preferred_element_type=jnp.float32)  25 us
  transfers between devices with their start and end apart: 66, of which 4 were waited for; matrix products, arithmetic and copies ran while one was open for 18% of the time, Pallas kernels for 0%

profile of v1, /device:TPU:8, one launch (start us, length us, event | category | flops | bytes accessed | tf_op | source)
XLA Modules:
  0.0 796.1 jit_solution(14250210740742902634)
XLA Ops:
  10.0 8.6 %copy.93 = bf16[1136,2272]{0,1:T(8,128)(2,1)} copy(bf16[1136,2272]{1,0:T(8,128)(2,1)} %param.33) | data formatting | bytes 10323968 | tf_op args[10]
  18.7 4.4 all_gather.96
  24.0 30.8 %all_gather.97 = bf16[4,2,4544]{0,1,2:T(2,128)(2,1)S(1)} all-gather(bf16[4,2,284]{0,1,2:T(2,128)(2,1)S(1)} %copy.84), channel_id=1, replica_groups=mesh['req'=2,'seq'=16] {'seq'}, dimensions={2}, use_global_device_ids=true | all-gather | bytes 77248 | tf_op jit(solution)/shard_map/all_gather | solution.py:93
  54.8 10.2 %fusion.185 = (bf16[1,2,4544]{0,1,2:T(2,128)(2,1)S(1)}, bf16[1,2,4544]{0,1,2:T(2,128)(2,1)}, f32[1,2,4544]{0,1,2:T(2,128)}, bf16[1,2,4544]{0,1,2:T(2,128)(2,1)}) fusion(bf16[4,2,4544]{0,1,2:T(2,128)(2,1)S(1)} %all_gather.97), kind=kLoop, calls=%fused_computation.373 | loop fusion | flops 9088 | bytes 163584 | tf_op jit(solution)/shard_map/slice | solution.py:109
  65.0 5.3 fusion.48
  70.9 5.5 copy.105
  77.9 5.1 copy.133
  84.0 5.1 copy.132
  100.2 6.0 copy.92
  106.2 5.7 reshape.545
  111.9 3.0 copy.94
  114.9 3.9 copy.116
  118.9 127.4 %all-gather.30.cloned.1.call-done = bf16[4544,1136]{1,0:T(8,128)(2,1)} async-done(((bf16[2272,1136]{1,0:T(8,128)(2,1)}), bf16[4544,1136]{1,0:T(8,128)(2,1)}) %all-gather.30.cloned.1.call-update) | async-done | bytes 10323984 | tf_op jit(solution)/shard_map/all_gather | solution.py:97
  246.2 25.6 %concatenate.141 = bf16[4544,1548]{1,0:T(8,128)(2,1)} concatenate(bf16[4544,284]{1,0:T(8,128)(2,1)S(1)} %bitcast.248, bf16[4544,128]{1,0:T(8,128)(2,1)} %all-gather.28.cloned.1.call-done, bf16[4544,1136]{1,0:T(8,128)(2,1)} %all-gather.30.cloned.1.call-done), dimensions={1} | concatenate | bytes 28136448 | tf_op jit(solution)/shard_map/concatenate | solution.py:101
  271.8 7.6 fusion.187
  286.3 2.8 collective-permute-start.53
  295.0 2.6 collective-permute-start.8
  300.4 2.6 collective-permute-start.39
  303.2 2.6 collective-permute-start.54
  305.8 2.6 collective-permute-start.9
  308.5 2.6 collective-permute-start.24
  311.2 3.5 collective-permute-start.40
  314.7 4.5 collective-permute-start.55
  319.3 4.4 collective-permute-start.10
  323.7 4.4 collective-permute-start.25
  328.1 4.4 collective-permute-start.41
  332.6 4.4 collective-permute-start.56
  337.1 4.5 collective-permute-start.11
  341.8 4.4 collective-permute-start.26
  346.1 4.4 collective-permute-start.42
  350.6 4.4 collective-permute-start.57
  355.2 4.4 collective-permute-start.12
  359.6 4.5 collective-permute-start.27
  364.3 4.4 collective-permute-start.43
  368.7 4.4 collective-permute-start.58
  373.4 4.4 collective-permute-start.13
  377.8 4.4 collective-permute-start.44
  382.3 4.4 collective-permute-start.28
  386.8 4.4 collective-permute-start.59
  391.8 4.5 collective-permute-start.14
  396.3 4.4 collective-permute-start.29
  403.5 2.8 collective-permute-done.7
  408.1 24.3 %all-gather.20 = f32[16,2,71]{2,1,0:T(2,128)S(1)} all-gather(f32[1,2,71]{2,1,0:T(2,128)S(1)} %bitcast.258), channel_id=11, replica_groups=mesh['req'=2,'seq'=16] {'seq'}, dimensions={0}, use_global_device_ids=true | all-gather | bytes 9656 | tf_op jit(solution)/shard_map/all_gather | solution.py:25
  432.4 17.5 %all-gather.21 = f32[16,2,71]{2,1,0:T(2,128)S(1)} all-gather(f32[1,2,71]{2,1,0:T(2,128)S(1)} %bitcast.262), channel_id=12, replica_groups=mesh['req'=2,'seq'=16] {'seq'}, dimensions={0}, use_global_device_ids=true | all-gather | bytes 9656 | tf_op jit(solution)/shard_map/all_gather | solution.py:25
  449.9 22.0 %all-gather.11 = f32[32,71,64]{1,2,0:T(8,128)S(1)} all-gather(f32[2,71,64]{1,2,0:T(8,128)S(1)} %fusion.18), channel_id=13, replica_groups=mesh['req'=2,'seq'=16] {'seq'}, dimensions={0}, use_global_device_ids=true | all-gather | bytes 617984 | tf_op jit(solution)/shard_map/all_gather | solution.py:25
  472.0 4.4 while.79
  476.4 17.9 %all-gather.18 = f32[16,2,71]{2,1,0:T(2,128)S(1)} all-gather(f32[1,2,71]{2,1,0:T(2,128)S(1)} %bitcast.257), channel_id=8, replica_groups=mesh['req'=2,'seq'=16] {'seq'}, dimensions={0}, use_global_device_ids=true | all-gather | bytes 9656 | tf_op jit(solution)/shard_map/all_gather | solution.py:25
  494.3 18.1 %all-gather.19 = f32[16,2,71]{2,1,0:T(2,128)S(1)} all-gather(f32[1,2,71]{2,1,0:T(2,128)S(1)} %bitcast.261), channel_id=9, replica_groups=mesh['req'=2,'seq'=16] {'seq'}, dimensions={0}, use_global_device_ids=true | all-gather | bytes 9656 | tf_op jit(solution)/shard_map/all_gather | solution.py:25
  512.4 21.3 %all-gather.8 = f32[32,71,64]{1,2,0:T(8,128)S(1)} all-gather(f32[2,71,64]{1,2,0:T(8,128)S(1)} %fusion.16), channel_id=10, replica_groups=mesh['req'=2,'seq'=16] {'seq'}, dimensions={0}, use_global_device_ids=true | all-gather | bytes 617984 | tf_op jit(solution)/shard_map/all_gather | solution.py:25
  533.9 4.4 while.78
  538.3 18.2 %all-gather.16 = f32[16,2,71]{2,1,0:T(2,128)S(1)} all-gather(f32[1,2,71]{2,1,0:T(2,128)S(1)} %bitcast.256), channel_id=5, replica_groups=mesh['req'=2,'seq'=16] {'seq'}, dimensions={0}, use_global_device_ids=true | all-gather | bytes 9656 | tf_op jit(solution)/shard_map/all_gather | solution.py:25
  556.5 17.8 %all-gather.17 = f32[16,2,71]{2,1,0:T(2,128)S(1)} all-gather(f32[1,2,71]{2,1,0:T(2,128)S(1)} %bitcast.260), channel_id=6, replica_groups=mesh['req'=2,'seq'=16] {'seq'}, dimensions={0}, use_global_device_ids=true | all-gather | bytes 9656 | tf_op jit(solution)/shard_map/all_gather | solution.py:25
  574.4 21.6 %all-gather.5 = f32[32,71,64]{1,2,0:T(8,128)S(1)} all-gather(f32[2,71,64]{1,2,0:T(8,128)S(1)} %fusion.14), channel_id=7, replica_groups=mesh['req'=2,'seq'=16] {'seq'}, dimensions={0}, use_global_device_ids=true | all-gather | bytes 617984 | tf_op jit(solution)/shard_map/all_gather | solution.py:25
  596.1 4.4 while.77
  601.9 21.6 %all-gather.2 = f32[32,71,64]{1,2,0:T(8,128)S(1)} all-gather(f32[2,71,64]{1,2,0:T(8,128)S(1)} %fusion.12), channel_id=4, replica_groups=mesh['req'=2,'seq'=16] {'seq'}, dimensions={0}, use_global_device_ids=true | all-gather | bytes 617984 | tf_op jit(solution)/shard_map/all_gather | solution.py:25
  623.6 18.1 %all-gather.13 = f32[16,2,71]{2,1,0:T(2,128)S(1)} all-gather(f32[1,2,71]{2,1,0:T(2,128)S(1)} %bitcast.259), channel_id=2, replica_groups=mesh['req'=2,'seq'=16] {'seq'}, dimensions={0}, use_global_device_ids=true | all-gather | bytes 9656 | tf_op jit(solution)/shard_map/all_gather | solution.py:25
  641.9 17.7 %all-gather.14 = f32[16,2,71]{2,1,0:T(2,128)S(1)} all-gather(f32[1,2,71]{2,1,0:T(2,128)S(1)} %bitcast.263), channel_id=3, replica_groups=mesh['req'=2,'seq'=16] {'seq'}, dimensions={0}, use_global_device_ids=true | all-gather | bytes 9656 | tf_op jit(solution)/shard_map/all_gather | solution.py:25
  659.6 4.4 while.76
  664.5 10.6 %fusion.144 = f32[2,4544]{1,0:T(2,128)} fusion(bf16[2,1136]{1,0:T(2,128)(2,1)S(1)} %copy-done.33, bf16[2,284]{1,0:T(2,128)(2,1)S(1)} %constant_dynamic-slice_fusion.8, bf16[1136,4544]{0,1:T(8,128)(2,1)} %all-gather.32.cloned.1.call-done, bf16[284,4544]{0,1:T(8,128)(2,1)} %copy.94), kind=kOutput, calls=%fused_computation.244 | convolution fusion | flops 51631200 | bytes 12946992 | tf_op jit(solution)/shard_map/dot_general | solution.py:146
  675.2 4.8 fusion.140
  680.0 4.8 fusion.136
  684.8 4.8 fusion.132
  691.5 88.7 %all-reduce.7.cloned.1.call-done = (f32[2,4544]{1,0:T(2,128)}, f32[2,4544]{1,0:T(2,128)}, f32[2,4544]{1,0:T(2,128)}, f32[2,4544]{1,0:T(2,128)}) async-done(((f32[2,4544]{1,0:T(2,128)}, f32[2,4544]{1,0:T(2,128)}, f32[2,4544]{1,0:T(2,128)}, f32[2,4544]{1,0:T(2,128)}), (f32[2,4544]{1,0:T(2,128)}, f32[2,4544]{1,0:T(2,128)}, f32[2,4544]{1,0:T(2,128)}, f32[2,4544]{1,0:T(2,128)})) %all-reduce.7.cloned.1.call-update) | async-done | bytes 145424
  783.2 4.4 all_gather.127
  (588 shorter events, 62.9 us)
Async XLA Ops:
  7.2 93.0 %all-gather.36.cloned.1.call-start = ((), (), s32[]{:S(2)}) async-start(), calls=%async_computation.4 | async-start | bytes 3981312 | tf_op jit(solution)/shard_map/all_gather | solution.py:98
  7.9 107.0 %all-gather.34.cloned.1.call-start = ((), (), s32[]{:S(2)}) async-start(), calls=%async_computation.3 | async-start | bytes 3981312 | tf_op jit(solution)/shard_map/all_gather | solution.py:95
  8.7 110.2 %all-gather.28.cloned.1.call-start = ((), (), s32[]{:S(2)}) async-start(), calls=%async_computation | async-start | bytes 1744896 | tf_op jit(solution)/shard_map/all_gather | solution.py:96
  9.4 236.8 %all-gather.30.cloned.1.call-start = ((), (), s32[]{:S(2)}) async-start(), calls=%async_computation.1 | async-start | bytes 15704064 | tf_op jit(solution)/shard_map/all_gather | solution.py:97
  10.0 654.5 %all-gather.32.cloned.1.call-start = ((), (), s32[]{:S(2)}) async-start(), calls=%async_computation.2 | async-start | bytes 15704064 | tf_op jit(solution)/shard_map/all_gather | solution.py:99
  18.6 761.5 %all-reduce.7.cloned.1.call-start = ((), (), s32[]{:S(2)}) async-start(), calls=%async_computation.5 | async-start | bytes 294912
  283.6 11.5 %collective-permute-start.30 = (bf16[2,284]{1,0:T(2,128)(2,1)S(1)}, bf16[2,284]{1,0:T(2,128)(2,1)S(1)}, u32[]{:S(2)}, u32[]{:S(2)}) collective-permute-start(bf16[2,284]{1,0:T(2,128)(2,1)S(1)} %slice.278), channel_id=1, source_target_pairs={{0,1},{1,2},{2,3},{3,4},{4,5},{5,6},{6,7},{7,8},{8,9},{9,10},{10,1... | collective-permute-start | bytes 3416 | tf_op jit(solution)/shard_map/ppermute | solution.py:17
  283.6 14.1 %collective-permute-start.38 = (bf16[2,284]{1,0:T(2,128)(2,1)S(1)}, bf16[2,284]{1,0:T(2,128)(2,1)S(1)}, u32[]{:S(2)}, u32[]{:S(2)}) collective-permute-start(bf16[2,284]{1,0:T(2,128)(2,1)S(1)} %slice.278), channel_id=1, source_target_pairs={{0,15},{1,0},{2,1},{3,2},{4,3},{5,4},{6,5},{7,6},{8,7},{9,8},{10,9... | collective-permute-start | bytes 3416 | tf_op jit(solution)/shard_map/ppermute | solution.py:19
  286.3 11.5 %collective-permute-start.45 = (bf16[2,284]{1,0:T(2,128)(2,1)S(1)}, bf16[2,284]{1,0:T(2,128)(2,1)S(1)}, u32[]{:S(2)}, u32[]{:S(2)}) collective-permute-start(bf16[2,284]{1,0:T(2,128)(2,1)S(1)} %slice.291), channel_id=1, source_target_pairs={{0,1},{1,2},{2,3},{3,4},{4,5},{5,6},{6,7},{7,8},{8,9},{9,10},{10,1... | collective-permute-start | bytes 3416 | tf_op jit(solution)/shard_map/ppermute | solution.py:17
  286.3 14.2 %collective-permute-start.53 = (bf16[2,284]{1,0:T(2,128)(2,1)S(1)}, bf16[2,284]{1,0:T(2,128)(2,1)S(1)}, u32[]{:S(2)}, u32[]{:S(2)}) collective-permute-start(bf16[2,284]{1,0:T(2,128)(2,1)S(1)} %slice.291), channel_id=1, source_target_pairs={{0,15},{1,0},{2,1},{3,2},{4,3},{5,4},{6,5},{7,6},{8,7},{9,8},{10,9... | collective-permute-start | bytes 3416 | tf_op jit(solution)/shard_map/ppermute | solution.py:19
  294.6 5.8 collective-permute-start
  295.0 8.0 %collective-permute-start.8 = (bf16[2,284]{1,0:T(2,128)(2,1)S(1)}, bf16[2,284]{1,0:T(2,128)(2,1)S(1)}, u32[]{:S(2)}, u32[]{:S(2)}) collective-permute-start(bf16[2,284]{1,0:T(2,128)(2,1)S(1)} %slice.252), channel_id=1, source_target_pairs={{0,15},{1,0},{2,1},{3,2},{4,3},{5,4},{6,5},{7,6},{8,7},{9,8},{10,9... | collective-permute-start | bytes 3416 | tf_op jit(solution)/shard_map/ppermute | solution.py:19
  297.8 5.4 collective-permute-start.15
  297.8 8.0 %collective-permute-start.23 = (bf16[2,284]{1,0:T(2,128)(2,1)S(1)}, bf16[2,284]{1,0:T(2,128)(2,1)S(1)}, u32[]{:S(2)}, u32[]{:S(2)}) collective-permute-start(bf16[2,284]{1,0:T(2,128)(2,1)S(1)} %slice.265), channel_id=1, source_target_pairs={{0,15},{1,0},{2,1},{3,2},{4,3},{5,4},{6,5},{7,6},{8,7},{9,8},{10,9... | collective-permute-start | bytes 3416 | tf_op jit(solution)/shard_map/ppermute | solution.py:19
  300.4 8.0 %collective-permute-start.39 = (bf16[2,284]{1,0:T(2,128)(2,1)S(1)}, bf16[2,284]{1,0:T(2,128)(2,1)S(1)}, u32[]{:S(2)}, u32[]{:S(2)}) collective-permute-start(bf16[2,284]{1,0:T(2,128)(2,1)S(1)} %collective-permute-done.38), channel_id=1, source_target_pairs={{0,15},{1,0},{2,1},{3,2},{4,3},{5,4},{6,5},{7,6},{8,7},{9,8},{10,9... | collective-permute-start | bytes 3416 | tf_op jit(solution)/shard_map/ppermute | solution.py:19
  303.2 8.0 %collective-permute-start.54 = (bf16[2,284]{1,0:T(2,128)(2,1)S(1)}, bf16[2,284]{1,0:T(2,128)(2,1)S(1)}, u32[]{:S(2)}, u32[]{:S(2)}) collective-permute-start(bf16[2,284]{1,0:T(2,128)(2,1)S(1)} %collective-permute-done.53), channel_id=1, source_target_pairs={{0,15},{1,0},{2,1},{3,2},{4,3},{5,4},{6,5},{7,6},{8,7},{9,8},{10,9... | collective-permute-start | bytes 3416 | tf_op jit(solution)/shard_map/ppermute | solution.py:19
  305.8 5.4 collective-permute-start.1
  305.8 8.9 %collective-permute-start.9 = (bf16[2,284]{1,0:T(2,128)(2,1)S(1)}, bf16[2,284]{1,0:T(2,128)(2,1)S(1)}, u32[]{:S(2)}, u32[]{:S(2)}) collective-permute-start(bf16[2,284]{1,0:T(2,128)(2,1)S(1)} %collective-permute-done.8), channel_id=1, source_target_pairs={{0,15},{1,0},{2,1},{3,2},{4,3},{5,4},{6,5},{7,6},{8,7},{9,8},{10,9... | collective-permute-start | bytes 3416 | tf_op jit(solution)/shard_map/ppermute | solution.py:19
  308.5 6.2 collective-permute-start.16
  308.5 10.7 %collective-permute-start.24 = (bf16[2,284]{1,0:T(2,128)(2,1)S(1)}, bf16[2,284]{1,0:T(2,128)(2,1)S(1)}, u32[]{:S(2)}, u32[]{:S(2)}) collective-permute-start(bf16[2,284]{1,0:T(2,128)(2,1)S(1)} %collective-permute-done.23), channel_id=1, source_target_pairs={{0,15},{1,0},{2,1},{3,2},{4,3},{5,4},{6,5},{7,6},{8,7},{9,8},{10,9... | collective-permute-start | bytes 3416 | tf_op jit(solution)/shard_map/ppermute | solution.py:19
  311.2 8.1 %collective-permute-start.32 = (bf16[2,284]{1,0:T(2,128)(2,1)S(1)}, bf16[2,284]{1,0:T(2,128)(2,1)S(1)}, u32[]{:S(2)}, u32[]{:S(2)}) collective-permute-start(bf16[2,284]{1,0:T(2,128)(2,1)S(1)} %collective-permute-done.31), channel_id=1, source_target_pairs={{0,1},{1,2},{2,3},{3,4},{4,5},{5,6},{6,7},{7,8},{8,9},{9,10},{10,1... | collective-permute-start | bytes 3416 | tf_op jit(solution)/shard_map/ppermute | solution.py:17
  311.2 12.4 %collective-permute-start.40 = (bf16[2,284]{1,0:T(2,128)(2,1)S(1)}, bf16[2,284]{1,0:T(2,128)(2,1)S(1)}, u32[]{:S(2)}, u32[]{:S(2)}) collective-permute-start(bf16[2,284]{1,0:T(2,128)(2,1)S(1)} %collective-permute-done.39), channel_id=1, source_target_pairs={{0,15},{1,0},{2,1},{3,2},{4,3},{5,4},{6,5},{7,6},{8,7},{9,8},{10,9... | collective-permute-start | bytes 3416 | tf_op jit(solution)/shard_map/ppermute | solution.py:19
  314.7 9.0 %collective-permute-start.47 = (bf16[2,284]{1,0:T(2,128)(2,1)S(1)}, bf16[2,284]{1,0:T(2,128)(2,1)S(1)}, u32[]{:S(2)}, u32[]{:S(2)}) collective-permute-start(bf16[2,284]{1,0:T(2,128)(2,1)S(1)} %collective-permute-done.46), channel_id=1, source_target_pairs={{0,1},{1,2},{2,3},{3,4},{4,5},{5,6},{6,7},{7,8},{8,9},{9,10},{10,1... | collective-permute-start | bytes 3416 | tf_op jit(solution)/shard_map/ppermute | solution.py:17
  314.7 13.4 %collective-permute-start.55 = (bf16[2,284]{1,0:T(2,128)(2,1)S(1)}, bf16[2,284]{1,0:T(2,128)(2,1)S(1)}, u32[]{:S(2)}, u32[]{:S(2)}) collective-permute-start(bf16[2,284]{1,0:T(2,128)(2,1)S(1)} %collective-permute-done.54), channel_id=1, source_target_pairs={{0,15},{1,0},{2,1},{3,2},{4,3},{5,4},{6,5},{7,6},{8,7},{9,8},{10,9... | collective-permute-start | bytes 3416 | tf_op jit(solution)/shard_map/ppermute | solution.py:19
  319.2 8.9 %collective-permute-start.2 = (bf16[2,284]{1,0:T(2,128)(2,1)S(1)}, bf16[2,284]{1,0:T(2,128)(2,1)S(1)}, u32[]{:S(2)}, u32[]{:S(2)}) collective-permute-start(bf16[2,284]{1,0:T(2,128)(2,1)S(1)} %collective-permute-done.1), channel_id=1, source_target_pairs={{0,1},{1,2},{2,3},{3,4},{4,5},{5,6},{6,7},{7,8},{8,9},{9,10},{10,1... | collective-permute-start | bytes 3416 | tf_op jit(solution)/shard_map/ppermute | solution.py:17
  319.3 13.3 %collective-permute-start.10 = (bf16[2,284]{1,0:T(2,128)(2,1)S(1)}, bf16[2,284]{1,0:T(2,128)(2,1)S(1)}, u32[]{:S(2)}, u32[]{:S(2)}) collective-permute-start(bf16[2,284]{1,0:T(2,128)(2,1)S(1)} %collective-permute-done.9), channel_id=1, source_target_pairs={{0,15},{1,0},{2,1},{3,2},{4,3},{5,4},{6,5},{7,6},{8,7},{9,8},{10,9... | collective-permute-start | bytes 3416 | tf_op jit(solution)/shard_map/ppermute | solution.py:19
  323.7 9.0 %collective-permute-start.17 = (bf16[2,284]{1,0:T(2,128)(2,1)S(1)}, bf16[2,284]{1,0:T(2,128)(2,1)S(1)}, u32[]{:S(2)}, u32[]{:S(2)}) collective-permute-start(bf16[2,284]{1,0:T(2,128)(2,1)S(1)} %collective-permute-done.16), channel_id=1, source_target_pairs={{0,1},{1,2},{2,3},{3,4},{4,5},{5,6},{6,7},{7,8},{8,9},{9,10},{10,1... | collective-permute-start | bytes 3416 | tf_op jit(solution)/shard_map/ppermute | solution.py:17
  323.7 13.4 %collective-permute-start.25 = (bf16[2,284]{1,0:T(2,128)(2,1)S(1)}, bf16[2,284]{1,0:T(2,128)(2,1)S(1)}, u32[]{:S(2)}, u32[]{:S(2)}) collective-permute-start(bf16[2,284]{1,0:T(2,128)(2,1)S(1)} %collective-permute-done.24), channel_id=1, source_target_pairs={{0,15},{1,0},{2,1},{3,2},{4,3},{5,4},{6,5},{7,6},{8,7},{9,8},{10,9... | collective-permute-start | bytes 3416 | tf_op jit(solution)/shard_map/ppermute | solution.py:19
  328.1 9.0 %collective-permute-start.33 = (bf16[2,284]{1,0:T(2,128)(2,1)S(1)}, bf16[2,284]{1,0:T(2,128)(2,1)S(1)}, u32[]{:S(2)}, u32[]{:S(2)}) collective-permute-start(bf16[2,284]{1,0:T(2,128)(2,1)S(1)} %collective-permute-done.32), channel_id=1, source_target_pairs={{0,1},{1,2},{2,3},{3,4},{4,5},{5,6},{6,7},{7,8},{8,9},{9,10},{10,1... | collective-permute-start | bytes 3416 | tf_op jit(solution)/shard_map/ppermute | solution.py:17
  328.1 13.5 %collective-permute-start.41 = (bf16[2,284]{1,0:T(2,128)(2,1)S(1)}, bf16[2,284]{1,0:T(2,128)(2,1)S(1)}, u32[]{:S(2)}, u32[]{:S(2)}) collective-permute-start(bf16[2,284]{1,0:T(2,128)(2,1)S(1)} %collective-permute-done.40), channel_id=1, source_target_pairs={{0,15},{1,0},{2,1},{3,2},{4,3},{5,4},{6,5},{7,6},{8,7},{9,8},{10,9... | collective-permute-start | bytes 3416 | tf_op jit(solution)/shard_map/ppermute | solution.py:19
  332.6 9.1 %collective-permute-start.48 = (bf16[2,284]{1,0:T(2,128)(2,1)S(1)}, bf16[2,284]{1,0:T(2,128)(2,1)S(1)}, u32[]{:S(2)}, u32[]{:S(2)}) collective-permute-start(bf16[2,284]{1,0:T(2,128)(2,1)S(1)} %collective-permute-done.47), channel_id=1, source_target_pairs={{0,1},{1,2},{2,3},{3,4},{4,5},{5,6},{6,7},{7,8},{8,9},{9,10},{10,1... | collective-permute-start | bytes 3416 | tf_op jit(solution)/shard_map/ppermute | solution.py:17
  332.6 13.5 %collective-permute-start.56 = (bf16[2,284]{1,0:T(2,128)(2,1)S(1)}, bf16[2,284]{1,0:T(2,128)(2,1)S(1)}, u32[]{:S(2)}, u32[]{:S(2)}) collective-permute-start(bf16[2,284]{1,0:T(2,128)(2,1)S(1)} %collective-permute-done.55), channel_id=1, source_target_pairs={{0,15},{1,0},{2,1},{3,2},{4,3},{5,4},{6,5},{7,6},{8,7},{9,8},{10,9... | collective-permute-start | bytes 3416 | tf_op jit(solution)/shard_map/ppermute | solution.py:19
  337.1 9.1 %collective-permute-start.3 = (bf16[2,284]{1,0:T(2,128)(2,1)S(1)}, bf16[2,284]{1,0:T(2,128)(2,1)S(1)}, u32[]{:S(2)}, u32[]{:S(2)}) collective-permute-start(bf16[2,284]{1,0:T(2,128)(2,1)S(1)} %collective-permute-done.2), channel_id=1, source_target_pairs={{0,1},{1,2},{2,3},{3,4},{4,5},{5,6},{6,7},{7,8},{8,9},{9,10},{10,1... | collective-permute-start | bytes 3416 | tf_op jit(solution)/shard_map/ppermute | solution.py:17
  337.1 13.5 %collective-permute-start.11 = (bf16[2,284]{1,0:T(2,128)(2,1)S(1)}, bf16[2,284]{1,0:T(2,128)(2,1)S(1)}, u32[]{:S(2)}, u32[]{:S(2)}) collective-permute-start(bf16[2,284]{1,0:T(2,128)(2,1)S(1)} %collective-permute-done.10), channel_id=1, source_target_pairs={{0,15},{1,0},{2,1},{3,2},{4,3},{5,4},{6,5},{7,6},{8,7},{9,8},{10,9... | collective-permute-start | bytes 3416 | tf_op jit(solution)/shard_map/ppermute | solution.py:19
  341.6 9.0 %collective-permute-start.18 = (bf16[2,284]{1,0:T(2,128)(2,1)S(1)}, bf16[2,284]{1,0:T(2,128)(2,1)S(1)}, u32[]{:S(2)}, u32[]{:S(2)}) collective-permute-start(bf16[2,284]{1,0:T(2,128)(2,1)S(1)} %collective-permute-done.17), channel_id=1, source_target_pairs={{0,1},{1,2},{2,3},{3,4},{4,5},{5,6},{6,7},{7,8},{8,9},{9,10},{10,1... | collective-permute-start | bytes 3416 | tf_op jit(solution)/shard_map/ppermute | solution.py:17
  341.8 13.4 %collective-permute-start.26 = (bf16[2,284]{1,0:T(2,128)(2,1)S(1)}, bf16[2,284]{1,0:T(2,128)(2,1)S(1)}, u32[]{:S(2)}, u32[]{:S(2)}) collective-permute-start(bf16[2,284]{1,0:T(2,128)(2,1)S(1)} %collective-permute-done.25), channel_id=1, source_target_pairs={{0,15},{1,0},{2,1},{3,2},{4,3},{5,4},{6,5},{7,6},{8,7},{9,8},{10,9... | collective-permute-start | bytes 3416 | tf_op jit(solution)/shard_map/ppermute | solution.py:19
  346.1 9.1 %collective-permute-start.34 = (bf16[2,284]{1,0:T(2,128)(2,1)S(1)}, bf16[2,284]{1,0:T(2,128)(2,1)S(1)}, u32[]{:S(2)}, u32[]{:S(2)}) collective-permute-start(bf16[2,284]{1,0:T(2,128)(2,1)S(1)} %collective-permute-done.33), channel_id=1, source_target_pairs={{0,1},{1,2},{2,3},{3,4},{4,5},{5,6},{6,7},{7,8},{8,9},{9,10},{10,1... | collective-permute-start | bytes 3416 | tf_op jit(solution)/shard_map/ppermute | solution.py:17
  346.1 13.5 %collective-permute-start.42 = (bf16[2,284]{1,0:T(2,128)(2,1)S(1)}, bf16[2,284]{1,0:T(2,128)(2,1)S(1)}, u32[]{:S(2)}, u32[]{:S(2)}) collective-permute-start(bf16[2,284]{1,0:T(2,128)(2,1)S(1)} %collective-permute-done.41), channel_id=1, source_target_pairs={{0,15},{1,0},{2,1},{3,2},{4,3},{5,4},{6,5},{7,6},{8,7},{9,8},{10,9... | collective-permute-start | bytes 3416 | tf_op jit(solution)/shard_map/ppermute | solution.py:19
  350.6 9.1 %collective-permute-start.49 = (bf16[2,284]{1,0:T(2,128)(2,1)S(1)}, bf16[2,284]{1,0:T(2,128)(2,1)S(1)}, u32[]{:S(2)}, u32[]{:S(2)}) collective-permute-start(bf16[2,284]{1,0:T(2,128)(2,1)S(1)} %collective-permute-done.48), channel_id=1, source_target_pairs={{0,1},{1,2},{2,3},{3,4},{4,5},{5,6},{6,7},{7,8},{8,9},{9,10},{10,1... | collective-permute-start | bytes 3416 | tf_op jit(solution)/shard_map/ppermute | solution.py:17
  350.6 13.5 %collective-permute-start.57 = (bf16[2,284]{1,0:T(2,128)(2,1)S(1)}, bf16[2,284]{1,0:T(2,128)(2,1)S(1)}, u32[]{:S(2)}, u32[]{:S(2)}) collective-permute-start(bf16[2,284]{1,0:T(2,128)(2,1)S(1)} %collective-permute-done.56), channel_id=1, source_target_pairs={{0,15},{1,0},{2,1},{3,2},{4,3},{5,4},{6,5},{7,6},{8,7},{9,8},{10,9... | collective-permute-start | bytes 3416 | tf_op jit(solution)/shard_map/ppermute | solution.py:19
  355.2 9.1 %collective-permute-start.4 = (bf16[2,284]{1,0:T(2,128)(2,1)S(1)}, bf16[2,284]{1,0:T(2,128)(2,1)S(1)}, u32[]{:S(2)}, u32[]{:S(2)}) collective-permute-start(bf16[2,284]{1,0:T(2,128)(2,1)S(1)} %collective-permute-done.3), channel_id=1, source_target_pairs={{0,1},{1,2},{2,3},{3,4},{4,5},{5,6},{6,7},{7,8},{8,9},{9,10},{10,1... | collective-permute-start | bytes 3416 | tf_op jit(solution)/shard_map/ppermute | solution.py:17
  355.2 13.5 %collective-permute-start.12 = (bf16[2,284]{1,0:T(2,128)(2,1)S(1)}, bf16[2,284]{1,0:T(2,128)(2,1)S(1)}, u32[]{:S(2)}, u32[]{:S(2)}) collective-permute-start(bf16[2,284]{1,0:T(2,128)(2,1)S(1)} %collective-permute-done.11), channel_id=1, source_target_pairs={{0,15},{1,0},{2,1},{3,2},{4,3},{5,4},{6,5},{7,6},{8,7},{9,8},{10,9... | collective-permute-start | bytes 3416 | tf_op jit(solution)/shard_map/ppermute | solution.py:19
  359.6 9.0 %collective-permute-start.19 = (bf16[2,284]{1,0:T(2,128)(2,1)S(1)}, bf16[2,284]{1,0:T(2,128)(2,1)S(1)}, u32[]{:S(2)}, u32[]{:S(2)}) collective-permute-start(bf16[2,284]{1,0:T(2,128)(2,1)S(1)} %collective-permute-done.18), channel_id=1, source_target_pairs={{0,1},{1,2},{2,3},{3,4},{4,5},{5,6},{6,7},{7,8},{8,9},{9,10},{10,1... | collective-permute-start | bytes 3416 | tf_op jit(solution)/shard_map/ppermute | solution.py:17
  359.6 13.5 %collective-permute-start.27 = (bf16[2,284]{1,0:T(2,128)(2,1)S(1)}, bf16[2,284]{1,0:T(2,128)(2,1)S(1)}, u32[]{:S(2)}, u32[]{:S(2)}) collective-permute-start(bf16[2,284]{1,0:T(2,128)(2,1)S(1)} %collective-permute-done.26), channel_id=1, source_target_pairs={{0,15},{1,0},{2,1},{3,2},{4,3},{5,4},{6,5},{7,6},{8,7},{9,8},{10,9... | collective-permute-start | bytes 3416 | tf_op jit(solution)/shard_map/ppermute | solution.py:19
  364.1 9.0 %collective-permute-start.35 = (bf16[2,284]{1,0:T(2,128)(2,1)S(1)}, bf16[2,284]{1,0:T(2,128)(2,1)S(1)}, u32[]{:S(2)}, u32[]{:S(2)}) collective-permute-start(bf16[2,284]{1,0:T(2,128)(2,1)S(1)} %collective-permute-done.34), channel_id=1, source_target_pairs={{0,1},{1,2},{2,3},{3,4},{4,5},{5,6},{6,7},{7,8},{8,9},{9,10},{10,1... | collective-permute-start | bytes 3416 | tf_op jit(solution)/shard_map/ppermute | solution.py:17
  364.3 9.1 %collective-permute-start.43 = (bf16[2,284]{1,0:T(2,128)(2,1)S(1)}, bf16[2,284]{1,0:T(2,128)(2,1)S(1)}, u32[]{:S(2)}, u32[]{:S(2)}) collective-permute-start(bf16[2,284]{1,0:T(2,128)(2,1)S(1)} %collective-permute-done.42), channel_id=1, source_target_pairs={{0,15},{1,0},{2,1},{3,2},{4,3},{5,4},{6,5},{7,6},{8,7},{9,8},{10,9... | collective-permute-start | bytes 3416 | tf_op jit(solution)/shard_map/ppermute | solution.py:19
  368.7 9.1 %collective-permute-start.50 = (bf16[2,284]{1,0:T(2,128)(2,1)S(1)}, bf16[2,284]{1,0:T(2,128)(2,1)S(1)}, u32[]{:S(2)}, u32[]{:S(2)}) collective-permute-start(bf16[2,284]{1,0:T(2,128)(2,1)S(1)} %collective-permute-done.49), channel_id=1, source_target_pairs={{0,1},{1,2},{2,3},{3,4},{4,5},{5,6},{6,7},{7,8},{8,9},{9,10},{10,1... | collective-permute-start | bytes 3416 | tf_op jit(solution)/shard_map/ppermute | solution.py:17
  368.7 9.1 %collective-permute-start.58 = (bf16[2,284]{1,0:T(2,128)(2,1)S(1)}, bf16[2,284]{1,0:T(2,128)(2,1)S(1)}, u32[]{:S(2)}, u32[]{:S(2)}) collective-permute-start(bf16[2,284]{1,0:T(2,128)(2,1)S(1)} %collective-permute-done.57), channel_id=1, source_target_pairs={{0,15},{1,0},{2,1},{3,2},{4,3},{5,4},{6,5},{7,6},{8,7},{9,8},{10,9... | collective-permute-start | bytes 3416 | tf_op jit(solution)/shard_map/ppermute | solution.py:19
  373.1 9.1 %collective-permute-start.5 = (bf16[2,284]{1,0:T(2,128)(2,1)S(1)}, bf16[2,284]{1,0:T(2,128)(2,1)S(1)}, u32[]{:S(2)}, u32[]{:S(2)}) collective-permute-start(bf16[2,284]{1,0:T(2,128)(2,1)S(1)} %collective-permute-done.4), channel_id=1, source_target_pairs={{0,1},{1,2},{2,3},{3,4},{4,5},{5,6},{6,7},{7,8},{8,9},{9,10},{10,1... | collective-permute-start | bytes 3416 | tf_op jit(solution)/shard_map/ppermute | solution.py:17
  373.1 9.1 %collective-permute-start.36 = (bf16[2,284]{1,0:T(2,128)(2,1)S(1)}, bf16[2,284]{1,0:T(2,128)(2,1)S(1)}, u32[]{:S(2)}, u32[]{:S(2)}) collective-permute-start(bf16[2,284]{1,0:T(2,128)(2,1)S(1)} %collective-permute-done.35), channel_id=1, source_target_pairs={{0,1},{1,2},{2,3},{3,4},{4,5},{5,6},{6,7},{7,8},{8,9},{9,10},{10,1... | collective-permute-start | bytes 3416 | tf_op jit(solution)/shard_map/ppermute | solution.py:17
  373.4 9.0 %collective-permute-start.13 = (bf16[2,284]{1,0:T(2,128)(2,1)S(1)}, bf16[2,284]{1,0:T(2,128)(2,1)S(1)}, u32[]{:S(2)}, u32[]{:S(2)}) collective-permute-start(bf16[2,284]{1,0:T(2,128)(2,1)S(1)} %collective-permute-done.12), channel_id=1, source_target_pairs={{0,15},{1,0},{2,1},{3,2},{4,3},{5,4},{6,5},{7,6},{8,7},{9,8},{10,9... | collective-permute-start | bytes 3416 | tf_op jit(solution)/shard_map/ppermute | solution.py:19
  377.7 9.0 %collective-permute-start.20 = (bf16[2,284]{1,0:T(2,128)(2,1)S(1)}, bf16[2,284]{1,0:T(2,128)(2,1)S(1)}, u32[]{:S(2)}, u32[]{:S(2)}) collective-permute-start(bf16[2,284]{1,0:T(2,128)(2,1)S(1)} %collective-permute-done.19), channel_id=1, source_target_pairs={{0,1},{1,2},{2,3},{3,4},{4,5},{5,6},{6,7},{7,8},{8,9},{9,10},{10,1... | collective-permute-start | bytes 3416 | tf_op jit(solution)/shard_map/ppermute | solution.py:17
  377.8 13.4 %collective-permute-start.44 = (bf16[2,284]{1,0:T(2,128)(2,1)S(1)}, bf16[2,284]{1,0:T(2,128)(2,1)S(1)}, u32[]{:S(2)}, u32[]{:S(2)}) collective-permute-start(bf16[2,284]{1,0:T(2,128)(2,1)S(1)} %collective-permute-done.43), channel_id=1, source_target_pairs={{0,15},{1,0},{2,1},{3,2},{4,3},{5,4},{6,5},{7,6},{8,7},{9,8},{10,9... | collective-permute-start | bytes 3416 | tf_op jit(solution)/shard_map/ppermute | solution.py:19
  382.2 9.0 %collective-permute-start.51 = (bf16[2,284]{1,0:T(2,128)(2,1)S(1)}, bf16[2,284]{1,0:T(2,128)(2,1)S(1)}, u32[]{:S(2)}, u32[]{:S(2)}) collective-permute-start(bf16[2,284]{1,0:T(2,128)(2,1)S(1)} %collective-permute-done.50), channel_id=1, source_target_pairs={{0,1},{1,2},{2,3},{3,4},{4,5},{5,6},{6,7},{7,8},{8,9},{9,10},{10,1... | collective-permute-start | bytes 3416 | tf_op jit(solution)/shard_map/ppermute | solution.py:17
  382.2 9.1 %collective-permute-start.37 = (bf16[2,284]{1,0:T(2,128)(2,1)S(1)}, bf16[2,284]{1,0:T(2,128)(2,1)S(1)}, u32[]{:S(2)}, u32[]{:S(2)}) collective-permute-start(bf16[2,284]{1,0:T(2,128)(2,1)S(1)} %collective-permute-done.36), channel_id=1, source_target_pairs={{0,1},{1,2},{2,3},{3,4},{4,5},{5,6},{6,7},{7,8},{8,9},{9,10},{10,1... | collective-permute-start | bytes 3416 | tf_op jit(solution)/shard_map/ppermute | solution.py:17
  382.3 9.4 %collective-permute-start.28 = (bf16[2,284]{1,0:T(2,128)(2,1)S(1)}, bf16[2,284]{1,0:T(2,128)(2,1)S(1)}, u32[]{:S(2)}, u32[]{:S(2)}) collective-permute-start(bf16[2,284]{1,0:T(2,128)(2,1)S(1)} %collective-permute-done.27), channel_id=1, source_target_pairs={{0,15},{1,0},{2,1},{3,2},{4,3},{5,4},{6,5},{7,6},{8,7},{9,8},{10,9... | collective-permute-start | bytes 3416 | tf_op jit(solution)/shard_map/ppermute | solution.py:19
  386.8 9.5 %collective-permute-start.59 = (bf16[2,284]{1,0:T(2,128)(2,1)S(1)}, bf16[2,284]{1,0:T(2,128)(2,1)S(1)}, u32[]{:S(2)}, u32[]{:S(2)}) collective-permute-start(bf16[2,284]{1,0:T(2,128)(2,1)S(1)} %collective-permute-done.58), channel_id=1, source_target_pairs={{0,15},{1,0},{2,1},{3,2},{4,3},{5,4},{6,5},{7,6},{8,7},{9,8},{10,9... | collective-permute-start | bytes 3416 | tf_op jit(solution)/shard_map/ppermute | solution.py:19
  391.2 9.5 %collective-permute-start.6 = (bf16[2,284]{1,0:T(2,128)(2,1)S(1)}, bf16[2,284]{1,0:T(2,128)(2,1)S(1)}, u32[]{:S(2)}, u32[]{:S(2)}) collective-permute-start(bf16[2,284]{1,0:T(2,128)(2,1)S(1)} %collective-permute-done.5), channel_id=1, source_target_pairs={{0,1},{1,2},{2,3},{3,4},{4,5},{5,6},{6,7},{7,8},{8,9},{9,10},{10,1... | collective-permute-start | bytes 3416 | tf_op jit(solution)/shard_map/ppermute | solution.py:17
  391.2 9.5 %collective-permute-start.21 = (bf16[2,284]{1,0:T(2,128)(2,1)S(1)}, bf16[2,284]{1,0:T(2,128)(2,1)S(1)}, u32[]{:S(2)}, u32[]{:S(2)}) collective-permute-start(bf16[2,284]{1,0:T(2,128)(2,1)S(1)} %collective-permute-done.20), channel_id=1, source_target_pairs={{0,1},{1,2},{2,3},{3,4},{4,5},{5,6},{6,7},{7,8},{8,9},{9,10},{10,1... | collective-permute-start | bytes 3416 | tf_op jit(solution)/shard_map/ppermute | solution.py:17
  391.3 9.7 %collective-permute-start.52 = (bf16[2,284]{1,0:T(2,128)(2,1)S(1)}, bf16[2,284]{1,0:T(2,128)(2,1)S(1)}, u32[]{:S(2)}, u32[]{:S(2)}) collective-permute-start(bf16[2,284]{1,0:T(2,128)(2,1)S(1)} %collective-permute-done.51), channel_id=1, source_target_pairs={{0,1},{1,2},{2,3},{3,4},{4,5},{5,6},{6,7},{7,8},{8,9},{9,10},{10,1... | collective-permute-start | bytes 3416 | tf_op jit(solution)/shard_map/ppermute | solution.py:17
  391.8 11.7 %collective-permute-start.14 = (bf16[2,284]{1,0:T(2,128)(2,1)S(1)}, bf16[2,284]{1,0:T(2,128)(2,1)S(1)}, u32[]{:S(2)}, u32[]{:S(2)}) collective-permute-start(bf16[2,284]{1,0:T(2,128)(2,1)S(1)} %collective-permute-done.13), channel_id=1, source_target_pairs={{0,15},{1,0},{2,1},{3,2},{4,3},{5,4},{6,5},{7,6},{8,7},{9,8},{10,9... | collective-permute-start | bytes 3416 | tf_op jit(solution)/shard_map/ppermute | solution.py:19
  396.3 10.2 %collective-permute-start.29 = (bf16[2,284]{1,0:T(2,128)(2,1)S(1)}, bf16[2,284]{1,0:T(2,128)(2,1)S(1)}, u32[]{:S(2)}, u32[]{:S(2)}) collective-permute-start(bf16[2,284]{1,0:T(2,128)(2,1)S(1)} %collective-permute-done.28), channel_id=1, source_target_pairs={{0,15},{1,0},{2,1},{3,2},{4,3},{5,4},{6,5},{7,6},{8,7},{9,8},{10,9... | collective-permute-start | bytes 3416 | tf_op jit(solution)/shard_map/ppermute | solution.py:19
  400.7 5.7 collective-permute-start.7
  400.7 6.0 collective-permute-start.22
  (53 other events, 2449.4 us)
Sparse Core Ops, SparseCore 0:
  9.6 40.6 all-gather.35
  51.8 39.3 all-gather.33
  92.8 22.6 all-gather.27
  116.9 129.3 all-gather.29
  247.6 129.3 all-gather.31
  689.8 90.2 all-reduce.6
